TPU v7x, 256 devices: a whole 4x4x8 slice. The times are simulated.
256 devices in a mesh: tok: 64 (over y, z, core), head: 4 (over x).
Axes of the slice: x: 4, y: 4, z: 8, core: 2. Of those that a mesh axis runs over, the one named last changes fastest.
Arguments:
- hidden: bfloat16 [2048, 2048], P('tok', 'head'), may hold values from -24 to 24
- attn_gain: float32 [2048], replicated, may hold values from 0.1 to 1.9
- w_query: bfloat16 [2048, 3072], P(None, 'head'), may hold values from -0.125 to 0.125
- w_latent: bfloat16 [2048, 576], P('head'), may hold values from -0.125 to 0.125
- w_key_up: bfloat16 [16, 128, 512], P('head'), may hold values from -0.5 to 0.5
- w_value_up: bfloat16 [16, 512, 128], P('head'), may hold values from -1 to 1
- w_out: bfloat16 [2048, 2048], P('head'), may hold values from -0.125 to 0.125
- latent_cache: bfloat16 [638976, 576], P(('tok', 'head')), may hold values from -6 to 6
- cache_lengths: int32 [2048], P('tok'), may hold values from 144 to 2048, as said below
- request_slot: int32 [2048], P('tok'), may hold values from 0 to 2047, as said below
- ffn_gain: float32 [2048], P('head'), may hold values from 0.1 to 1.9
- w_router: bfloat16 [2048, 64], P('head'), may hold values from -0.25 to 0.25
- routes: int32 [2048, 6], P('tok'), may hold values from 0 to 63, all different within a row; in each aligned block of 32 rows (0 to 31, 32 to 63, ...) at most 6 rows name the same one
- expert_gate: bfloat16 [64, 2048, 1408], P('tok', None, 'head'), may hold values from -0.125 to 0.125
- expert_up: bfloat16 [64, 2048, 1408], P('tok', None, 'head'), may hold values from -0.125 to 0.125
- expert_down: bfloat16 [64, 1408, 2048], P('tok', 'head'), may hold values from -0.15625 to 0.15625
Outputs:
- new_entry: bfloat16 [2048, 576], P('tok')
- attended: bfloat16 [2048, 2048], P('tok', 'head')
- expert_mix: bfloat16 [2048, 2048], P('tok', 'head')
Inputs may be any that keep to these rules, and one draw needn't show every extreme that they name: `request_slot`: a permutation of the 2048 slots; slot s lies on owner s // 32, so every owner holds 32 slots; the requests of one device name at most 1 slots of one owner, and every device reaches that bound. `cache_lengths`: the caches of an owner's slots lie end to end in slot order at the start of that owner's 9984 rows of latent_cache; they fill at most 9984 rows, and some owner fills all of them. `routes`: each row names 6 different experts; in the rows of one device no expert is named more than 6 times.
All inputs are finite; a program needn't handle non-finite values.
Results may differ from a plain program's by a relative error of at most 0.028.
Values may be sent and summed in bfloat16 or wider, within the bound.
No kernel may reach another device: no remote copies, remote signals or barrier semaphores. Data moves between devices by JAX's collectives and lax.ppermute only.
A program may use at most 128 MiB of HBM per device.

v0:
```python
import jax
import jax.numpy as jnp
from jax import lax
from jax.sharding import PartitionSpec as P

D = 2048
NOPE = 128
ROPE = 64
LATENT = 512
NORM_EPS = 1e-06


def rotate_pairs(values, places):
    halfway = values.shape[-1] // 2
    freqs = 10000.0 ** (-jnp.arange(halfway, dtype=jnp.float32) / halfway)
    angles = places.astype(jnp.float32).reshape(places.shape + (1,) * (values.ndim - 1)) * freqs
    cosine = jnp.cos(angles)
    sine = jnp.sin(angles)
    first_half = values[..., :halfway]
    second_half = values[..., halfway:]
    return jnp.concatenate(
        [first_half * cosine - second_half * sine, first_half * sine + second_half * cosine],
        axis=-1,
    )


def owner_attend(all_heads, owner_lengths, latent_cache, head_index, factor):
    slot_rows = all_heads.shape[0]
    total_heads = all_heads.shape[1]
    probe_width = all_heads.shape[2]
    key_rows = latent_cache.shape[0]
    starts = jnp.cumsum(owner_lengths) - owner_lengths
    places = head_index * key_rows + jnp.arange(key_rows, dtype=jnp.int32)
    inside = (places[None, :] >= starts[:, None]) & (
        places[None, :] < (starts + owner_lengths)[:, None]
    )
    scores = factor * jnp.einsum(
        "qc,pc->qp",
        all_heads.reshape(slot_rows * total_heads, probe_width),
        latent_cache,
        preferred_element_type=jnp.float32,
    )
    scores = scores.reshape(slot_rows, total_heads, key_rows)
    weights = jnp.where(inside[:, None, :], jnp.exp(scores), 0.0).astype(jnp.bfloat16)
    numerator = jnp.einsum(
        "khp,pl->khl", weights, latent_cache[:, :LATENT], preferred_element_type=jnp.float32
    )
    denominator = jnp.sum(weights.astype(jnp.float32), axis=2)
    return (numerator, denominator)


def head_sum_scatter(values, axis):
    groups = lax.axis_size("head")
    moved = lax.all_to_all(values, "head", split_axis=axis, concat_axis=0, tiled=True)
    moved = moved.reshape((groups, values.shape[0]) + moved.shape[1:])
    return jnp.sum(moved.astype(jnp.float32), axis=0)


def body(
    hidden,
    attn_gain,
    w_query,
    w_latent,
    w_key_up,
    w_value_up,
    w_out,
    latent_cache,
    cache_lengths,
    request_slot,
    ffn_gain,
    w_router,
    routes,
    expert_gate,
    expert_up,
    expert_down,
):
    local_rows = hidden.shape[0]
    quarter_width = hidden.shape[1]
    local_heads = w_key_up.shape[0]
    peer_count = lax.axis_size("tok")
    head_index = lax.axis_index("head")
    tok_index = lax.axis_index("tok")
    row_ids = jnp.arange(local_rows, dtype=jnp.int32)
    latent_width = w_latent.shape[1]
    head_count = lax.axis_size("head")
    gain_part = lax.dynamic_slice_in_dim(attn_gain, head_index * quarter_width, quarter_width, 0)
    raw_part = jnp.dot(
        (hidden.astype(jnp.float32) * gain_part).astype(jnp.bfloat16),
        w_latent,
        preferred_element_type=jnp.float32,
    )
    part_width = -(-latent_width // 128) * 128
    part_hi = lax.reduce_precision(raw_part, exponent_bits=8, mantissa_bits=7)
    rest = raw_part - part_hi
    part_mid = lax.reduce_precision(rest, exponent_bits=8, mantissa_bits=7)
    part_lo = rest - part_mid
    lane_pad = jnp.zeros((local_rows, part_width - latent_width), jnp.bfloat16)
    send_rows = jnp.concatenate(
        [
            hidden,
            part_hi.astype(jnp.bfloat16),
            lane_pad,
            part_mid.astype(jnp.bfloat16),
            lane_pad,
            part_lo.astype(jnp.bfloat16),
            lane_pad,
        ],
        axis=1,
    )
    got_rows = lax.all_gather(send_rows, "head", axis=0, tiled=False)
    hidden_groups = got_rows[:, :, :quarter_width].astype(jnp.float32)

    def part_piece(k):
        offset = quarter_width + k * part_width
        return got_rows[:, :, offset : offset + latent_width].astype(jnp.float32)

    part_sums = part_piece(0) + part_piece(1) + part_piece(2)
    inv_attn = lax.rsqrt(
        jnp.sum(hidden_groups * hidden_groups, axis=(0, 2))[:, None] / D + NORM_EPS
    )
    normed_groups = (
        hidden_groups * inv_attn[None] * attn_gain.reshape(head_count, 1, quarter_width)
    ).astype(jnp.bfloat16)
    compressed = jnp.sum(part_sums, axis=0) * inv_attn
    latent_new = compressed[:, :LATENT]
    latent_new = latent_new * lax.rsqrt(
        jnp.mean(latent_new * latent_new, axis=1, keepdims=True) + NORM_EPS
    )
    new_entry = jnp.concatenate(
        [latent_new, rotate_pairs(compressed[:, LATENT:], cache_lengths)], axis=1
    ).astype(jnp.bfloat16)
    queries = jnp.einsum(
        "gbf,gfq->bq",
        normed_groups,
        w_query.reshape(head_count, quarter_width, w_query.shape[1]),
        preferred_element_type=jnp.float32,
    ).astype(jnp.bfloat16)
    queries = queries.reshape(local_rows, local_heads, NOPE + ROPE)
    absorbed = jnp.einsum(
        "bhn,hnl->bhl", queries[:, :, :NOPE], w_key_up, preferred_element_type=jnp.float32
    ).astype(jnp.bfloat16)
    turned = rotate_pairs(queries[:, :, NOPE:].astype(jnp.float32), cache_lengths).astype(
        jnp.bfloat16
    )
    probes = jnp.concatenate([absorbed, turned], axis=2)
    factor = (NOPE + ROPE) ** (-0.5)
    owner_ids = jnp.arange(peer_count, dtype=jnp.int32)
    dest_owner = request_slot // local_rows
    goes_to = dest_owner[None, :] == owner_ids[:, None]
    sent_any = jnp.max(goes_to.astype(jnp.int32), axis=1)
    sent_row = jnp.sum(jnp.where(goes_to, row_ids[None, :], 0), axis=1)
    sent_slot = request_slot[sent_row]
    sent_len = cache_lengths[sent_row]
    code = (
        jnp.stack(
            [sent_any, sent_slot // 64, sent_slot % 64, sent_len // 64, sent_len % 64], axis=1
        )
        * sent_any[:, None]
    )
    code_row = jnp.zeros((peer_count, probes.shape[2]), jnp.float32)
    code_row = code_row.at[:, :5].set(code.astype(jnp.float32)).astype(jnp.bfloat16)
    packed = jnp.concatenate(
        [probes[sent_row], new_entry[sent_row][:, None, :], code_row[:, None, :]], axis=1
    )
    got_packed = lax.all_to_all(packed, "tok", 0, 0, tiled=True)
    got_code = got_packed[:, local_heads + 1, :5].astype(jnp.float32).astype(jnp.int32)
    got_slot = jnp.where(got_code[:, 0] > 0, got_code[:, 1] * 64 + got_code[:, 2], -1)
    got_len = got_code[:, 3] * 64 + got_code[:, 4]
    local_slot = got_slot - tok_index * local_rows
    slot_sel = local_slot[None, :] == row_ids[:, None]
    src_of_slot = jnp.sum(jnp.where(slot_sel, owner_ids[None, :], 0), axis=1)
    owner_probes = got_packed[src_of_slot, :local_heads]
    owner_lengths = got_len[src_of_slot]
    owner_new = got_packed[src_of_slot, local_heads]
    all_heads = lax.all_gather(owner_probes, "head", axis=1, tiled=True)
    numerator, denominator = owner_attend(
        all_heads, owner_lengths, latent_cache, head_index, factor
    )
    den_t = denominator.T
    den_hi = lax.reduce_precision(den_t, exponent_bits=8, mantissa_bits=7)
    den_rest = den_t - den_hi
    den_mid = lax.reduce_precision(den_rest, exponent_bits=8, mantissa_bits=7)
    den_lo = den_rest - den_mid
    den_row = jnp.zeros((3, denominator.shape[1], LATENT), jnp.float32)
    den_row = den_row.at[:, :, : denominator.shape[0]].set(jnp.stack([den_hi, den_mid, den_lo]))
    moved = lax.all_to_all(
        jnp.concatenate([numerator, den_row], axis=0).astype(jnp.bfloat16),
        "head",
        split_axis=1,
        concat_axis=0,
        tiled=True,
    ).astype(jnp.float32)
    moved = moved.reshape((head_count, local_rows + 3) + moved.shape[1:])
    joined = jnp.sum(moved[:, :local_rows], axis=0)
    den_parts = moved[:, local_rows:, :, :local_rows]
    group_den = jnp.sum(den_parts[:, 0] + den_parts[:, 1] + den_parts[:, 2], axis=0).T
    self_score = factor * jnp.einsum(
        "bhc,bc->bh", owner_probes, owner_new, preferred_element_type=jnp.float32
    )
    self_weight = jnp.exp(self_score).astype(jnp.bfloat16).astype(jnp.float32)
    total_num = joined[:local_rows] + self_weight[:, :, None] * owner_new[:, None, :LATENT].astype(
        jnp.float32
    )
    total_den = group_den + self_weight
    mixed_latent = (total_num / total_den[:, :, None]).astype(jnp.bfloat16)
    owner_out = jnp.einsum(
        "bhl,hld->bhd", mixed_latent, w_value_up, preferred_element_type=jnp.float32
    ).astype(jnp.bfloat16)
    owner_out = owner_out.reshape(local_rows, local_heads * NOPE)
    owner_out = jnp.concatenate(
        [owner_out, jnp.zeros((1, local_heads * NOPE), jnp.bfloat16)], axis=0
    )
    back_valid = (local_slot >= 0) & (local_slot < local_rows)
    back_row = jnp.where(back_valid, local_slot, local_rows)
    head_out = lax.all_to_all(owner_out[back_row], "tok", 0, 0, tiled=True)[dest_owner]
    head_out = head_out.reshape(local_rows, local_heads * NOPE)
    attn_piece = head_sum_scatter(
        jnp.dot(head_out, w_out, preferred_element_type=jnp.float32).astype(jnp.bfloat16), 1
    )
    attended = (hidden.astype(jnp.float32) + attn_piece).astype(jnp.bfloat16)
    attended_wide = attended.astype(jnp.float32)
    gained = (attended_wide * ffn_gain).astype(jnp.bfloat16)
    squares, logit_part = lax.psum(
        (
            jnp.sum(attended_wide * attended_wide, axis=1),
            jnp.dot(gained, w_router, preferred_element_type=jnp.float32),
        ),
        "head",
    )
    inv_ffn = lax.rsqrt(squares / D + NORM_EPS)
    logits = logit_part * inv_ffn[:, None]
    normed_ffn = (attended_wide * ffn_gain * inv_ffn[:, None]).astype(jnp.bfloat16)
    expert_count = w_router.shape[1]
    route_count = routes.shape[1]
    expert_ids = jnp.arange(expert_count, dtype=jnp.int32)
    named = routes[:, :, None] == expert_ids[None, None, :]
    picked = jnp.sum(jnp.where(named, logits[:, None, :], 0.0), axis=2)
    lifted = jnp.exp(picked)
    route_weight = lifted / jnp.sum(lifted, axis=1, keepdims=True)
    struck = jnp.max(named.astype(jnp.int32), axis=1)
    earlier_hits = jnp.cumsum(struck, axis=0) - struck
    capacity = min(local_rows, max(2, 2 * local_rows * route_count // expert_count))
    route_place = routes * capacity + jnp.take_along_axis(earlier_hits, routes, axis=1)
    slot_total = expert_count * capacity
    slot_ids = jnp.arange(slot_total, dtype=jnp.int32)
    filled = route_place[None, :, :] == slot_ids[:, None, None]
    source_token = jnp.sum(
        jnp.where(filled, row_ids[None, :, None], 0), axis=(1, 2)
    ) + local_rows * (1 - jnp.max(filled.astype(jnp.int32), axis=(1, 2)))
    padded_rows = jnp.concatenate(
        [normed_ffn, jnp.zeros((1, normed_ffn.shape[1]), jnp.bfloat16)], axis=0
    )
    arrived = lax.all_to_all(
        padded_rows[source_token].reshape(expert_count, capacity, quarter_width),
        "tok",
        split_axis=0,
        concat_axis=0,
        tiled=True,
    )
    expert_in = lax.all_to_all(
        jnp.broadcast_to(
            arrived.reshape(1, peer_count * capacity, quarter_width),
            (head_count, peer_count * capacity, quarter_width),
        ),
        "head",
        split_axis=0,
        concat_axis=2,
        tiled=True,
    ).reshape(peer_count * capacity, head_count * quarter_width)
    gate_value = jnp.dot(expert_in, expert_gate[0], preferred_element_type=jnp.float32)
    up_value = jnp.dot(expert_in, expert_up[0], preferred_element_type=jnp.float32)
    activity = (jax.nn.silu(gate_value) * up_value).astype(jnp.bfloat16)
    expert_share = head_sum_scatter(
        jnp.dot(activity, expert_down[0], preferred_element_type=jnp.float32).astype(jnp.bfloat16),
        1,
    ).astype(jnp.bfloat16)
    returned = lax.all_to_all(
        expert_share.reshape(peer_count, capacity, quarter_width),
        "tok",
        split_axis=0,
        concat_axis=0,
        tiled=True,
    )
    chosen_rows = returned.reshape(slot_total, quarter_width)[route_place]
    expert_mix = jnp.sum(route_weight[:, :, None] * chosen_rows.astype(jnp.float32), axis=1).astype(
        jnp.bfloat16
    )
    return (new_entry, attended, expert_mix)


def solution(mesh):
    in_specs = (
        P("tok", "head"),
        P(),
        P(None, "head"),
        P("head", None),
        P("head", None, None),
        P("head", None, None),
        P("head", None),
        P(("tok", "head"), None),
        P("tok"),
        P("tok"),
        P("head"),
        P("head", None),
        P("tok", None),
        P("tok", None, "head"),
        P("tok", None, "head"),
        P("tok", "head", None),
    )
    out_specs = (P("tok", None), P("tok", "head"), P("tok", "head"))
    return jax.shard_map(body, mesh=mesh, in_specs=in_specs, out_specs=out_specs, check_vma=False)
```

profile of v0, /device:TPU:1, one launch (start us, length us, event | category | flops | bytes accessed | tf_op | source)
XLA Modules:
  0.0 299.2 jit_solution(14646686963028986328)
XLA Ops:
  10.4 12.5 %all-gather = bf16[128,2432]{1,0:T(8,128)(2,1)S(1)} all-gather(bf16[32,2432]{1,0:T(8,128)(2,1)S(1)} %concatenate.36), channel_id=2, replica_groups=mesh['tok'=64,'head'=4] {'head'}, dimensions={0}, use_global_device_ids=true | all-gather | bytes 778240 | tf_op jit(solution)/shard_map/all_gather | solution.py:110
  34.7 2.5 pad_maximum_fusion
  37.1 14.2 %all-to-all-start = ((bf16[64,6,576]{2,1,0:T(8,128)(2,1)}), bf16[64,6,576]{2,1,0:T(8,128)(2,1)}, u32[]{:S(2)}, u32[]{:S(2)}) async-start(bf16[64,6,576]{2,1,0:T(8,128)(2,1)} %pad_maximum_fusion), calls=%async_computation | async-start | bytes 1310720 | tf_op jit(solution)/shard_map/all_to_all | solution.py:165
  54.8 16.5 %all-to-all-done = bf16[64,6,576]{2,1,0:T(8,128)(2,1)} async-done(((bf16[64,6,576]{2,1,0:T(8,128)(2,1)}), bf16[64,6,576]{2,1,0:T(8,128)(2,1)}, u32[]{:S(2)}, u32[]{:S(2)}) %all-to-all-start) | async-done | bytes 442400 | tf_op jit(solution)/shard_map/all_to_all | solution.py:165
  73.7 1.9 copy.308
  75.7 1.8 gather_fusion.6
  77.4 2.1 gather_fusion.5
  79.6 12.1 %all_gather.11 = bf16[32,16,576]{2,0,1:T(8,128)(2,1)S(1)} all-gather(bf16[32,4,576]{2,0,1:T(8,128)(2,1)S(1)} %gather_fusion.5), channel_id=1, replica_groups=mesh['tok'=64,'head'=4] {'head'}, dimensions={1}, use_global_device_ids=true | all-gather | bytes 737280 | tf_op jit(solution)/shard_map/all_gather | solution.py:175
  93.9 4.5 %convert_reduce_fusion = (f32[512]{0:T(512)S(1)}, bf16[512,2496]{0,1:T(8,128)(2,1)}) fusion(pred[512,2496]{0,1:T(32,128)(4,1)S(1)} %copy.312, bf16[512,576]{1,0:T(8,128)(2,1)S(1)} %bitcast.144, bf16[2496,576]{0,1:T(8,128)(2,1)S(1)} %copy-done.12), kind=kOutput, calls=%fused_computation.13 | convolution fusion | flops 1478589952 | bytes 7301120 | tf_op jit(solution)/shard_map/qc,pc->qp/dot_general | solution.py:37
  98.6 4.4 %copy.310 = bf16[512,2496]{1,0:T(8,128)(2,1)} copy(bf16[512,2496]{0,1:T(8,128)(2,1)} %get-tuple-element.67) | data formatting | bytes 5111808 | tf_op jit(solution)/shard_map/exp | solution.py:44
  102.9 4.1 %fusion.10 = bf16[32,16,512]{2,1,0:T(8,128)(2,1)S(1)} fusion(bf16[2496,576]{0,1:T(8,128)(2,1)} %param.27, bf16[32,16,2496]{2,1,0:T(8,128)(2,1)} %bitcast.138, pred[32,2496]{1,0:T(8,128)(4,1)S(1)} %compare_and_fusion), kind=kOutput, calls=%fused_computation.29 | convolution fusion | flops 1310162944 | bytes 5847040 | tf_op jit(solution)/shard_map/khp,pl->khl/dot_general | solution.py:45
  108.3 4.2 %all-to-all-start.1 = ((bf16[35,16,512]{2,0,1:T(8,128)(2,1)}), bf16[35,16,512]{2,0,1:T(8,128)(2,1)}, u32[]{:S(2)}, u32[]{:S(2)}) async-start(bf16[35,16,512]{2,0,1:T(8,128)(2,1)} %copy.314), calls=%async_computation.1 | async-start | bytes 1310720 | tf_op jit(solution)/shard_map/all_to_all | solution.py:186
  114.0 6.6 %all-to-all-done.1 = bf16[35,16,512]{2,0,1:T(8,128)(2,1)} async-done(((bf16[35,16,512]{2,0,1:T(8,128)(2,1)}), bf16[35,16,512]{2,0,1:T(8,128)(2,1)}, u32[]{:S(2)}, u32[]{:S(2)}) %all-to-all-start.1) | async-done | bytes 573472 | tf_op jit(solution)/shard_map/all_to_all | solution.py:186
  127.8 9.3 %all-to-all-start.2 = ((bf16[64,2,256]{2,1,0:T(2,128)(2,1)}), bf16[64,2,256]{2,1,0:T(2,128)(2,1)S(1)}, u32[]{:S(2)}, u32[]{:S(2)}) async-start(bf16[64,2,256]{2,1,0:T(2,128)(2,1)} %reshape.670), calls=%async_computation.2 | async-start | bytes 131072 | tf_op jit(solution)/shard_map/all_to_all | solution.py:215
  137.9 9.1 %all-to-all-done.2 = bf16[64,2,256]{2,1,0:T(2,128)(2,1)S(1)} async-done(((bf16[64,2,256]{2,1,0:T(2,128)(2,1)}), bf16[64,2,256]{2,1,0:T(2,128)(2,1)S(1)}, u32[]{:S(2)}, u32[]{:S(2)}) %all-to-all-start.2) | async-done | bytes 65568 | tf_op jit(solution)/shard_map/all_to_all | solution.py:215
  147.7 2.1 convolution_convert_fusion.1
  150.4 3.3 %all-to-all-start.3 = ((bf16[32,4,512]{2,0,1:T(8,128)(2,1)}), bf16[32,4,512]{2,0,1:T(8,128)(2,1)S(1)}, u32[]{:S(2)}, u32[]{:S(2)}) async-start(bf16[32,4,512]{2,0,1:T(8,128)(2,1)} %bitcast.127), calls=%async_computation.3 | async-start | bytes 262144 | tf_op jit(solution)/shard_map/all_to_all | solution.py:54
  153.7 4.8 %all-to-all-done.3 = bf16[32,4,512]{2,0,1:T(8,128)(2,1)S(1)} async-done(((bf16[32,4,512]{2,0,1:T(8,128)(2,1)}), bf16[32,4,512]{2,0,1:T(8,128)(2,1)S(1)}, u32[]{:S(2)}, u32[]{:S(2)}) %all-to-all-start.3) | async-done | bytes 131104 | tf_op jit(solution)/shard_map/all_to_all | solution.py:54
  158.8 12.5 %all-reduce.6 = (f32[32]{0:T(128)S(1)}, f32[32,64]{1,0:T(8,128)}) all-reduce(f32[32]{0:T(128)S(1)} %get-tuple-element.37, f32[32,64]{1,0:T(8,128)S(1)} %fusion.56), channel_id=1, replica_groups=mesh['tok'=64,'head'=4] {'head'}, use_global_device_ids=true, to_apply=%region_14.15 | all-reduce | flops 2080 | bytes 16640 | tf_op jit(solution)/shard_map/psum | solution.py:223
  171.5 2.6 gather_fusion.9
  174.0 1.9 reshape.555
  175.9 27.4 %all_to_all.77 = bf16[64,6,512]{2,1,0:T(8,128)(2,1)} all-to-all(bf16[64,6,512]{2,1,0:T(8,128)(2,1)} %reshape.555), channel_id=1, replica_groups=mesh['tok'=64,'head'=4] {'tok'}, dimensions={0} | all-to-all | bytes 786432 | tf_op jit(solution)/shard_map/all_to_all | solution.py:253
  206.5 23.0 %all_to_all.78 = bf16[4,384,512]{1,2,0:T(8,128)(2,1)S(1)} all-to-all(bf16[4,384,512]{1,2,0:T(8,128)(2,1)S(1)} %broadcast_in_dim.157), channel_id=1, replica_groups=mesh['tok'=64,'head'=4] {'head'}, dimensions={0} | all-to-all | bytes 3145728 | tf_op jit(solution)/shard_map/all_to_all | solution.py:260
  232.4 5.5 %convolution_convert_fusion = bf16[384,2048]{1,0:T(8,128)(2,1)} fusion(bf16[1,352,2048]{2,1,0:T(8,128)(2,1)} %param.35, bf16[384,2048]{0,1:T(8,128)(2,1)} %bitcast.141, bf16[1,2048,352]{1,2,0:T(8,128)(2,1)} %param.34, f32[384,352]{0,1:T(8,128)} %fusion.8), kind=kOutput, calls=%fused_computation.16 | convolution fusion | flops 1108893696 | bytes 6569984 | tf_op jit(solution)/shard_map/dot_general | solution.py:274
  237.9 2.7 copy.357
  240.6 4.5 %all-to-all-start.6 = ((bf16[384,4,512]{2,0,1:T(8,128)(2,1)}), bf16[384,4,512]{2,0,1:T(8,128)(2,1)}, u32[]{:S(2)}, u32[]{:S(2)}) async-start(bf16[384,4,512]{2,0,1:T(8,128)(2,1)} %bitcast.131), calls=%async_computation.6 | async-start | bytes 3145728 | tf_op jit(solution)/shard_map/all_to_all | solution.py:54
  245.2 19.5 %all-to-all-done.6 = bf16[384,4,512]{2,0,1:T(8,128)(2,1)} async-done(((bf16[384,4,512]{2,0,1:T(8,128)(2,1)}), bf16[384,4,512]{2,0,1:T(8,128)(2,1)}, u32[]{:S(2)}, u32[]{:S(2)}) %all-to-all-start.6) | async-done | bytes 1572896 | tf_op jit(solution)/shard_map/all_to_all | solution.py:54
  264.7 1.8 reduce_sum.160
  267.4 8.1 %all-to-all-start.7 = ((bf16[64,6,512]{2,1,0:T(8,128)(2,1)}), bf16[64,6,512]{2,1,0:T(8,128)(2,1)}, u32[]{:S(2)}, u32[]{:S(2)}) async-start(bf16[64,6,512]{2,1,0:T(8,128)(2,1)} %reshape.557), calls=%async_computation.7 | async-start | bytes 1048576 | tf_op jit(solution)/shard_map/all_to_all | solution.py:277
  277.2 15.5 %all-to-all-done.7 = bf16[64,6,512]{2,1,0:T(8,128)(2,1)} async-done(((bf16[64,6,512]{2,1,0:T(8,128)(2,1)}), bf16[64,6,512]{2,1,0:T(8,128)(2,1)}, u32[]{:S(2)}, u32[]{:S(2)}) %all-to-all-start.7) | async-done | bytes 393248 | tf_op jit(solution)/shard_map/all_to_all | solution.py:277
  295.6 1.8 reshape.654
  297.3 1.9 multiply_reduce_fusion
  (155 shorter events, 53.5 us)
Async XLA Ops:
  0.6 23.1 %copy-start = (bf16[2048,768]{1,0:T(8,128)(2,1)S(1)}, bf16[2048,768]{1,0:T(8,128)(2,1)}, u32[]{:S(2)}) copy-start(bf16[2048,768]{1,0:T(8,128)(2,1)} %param.22) | copy-start | bytes 9437188
  0.6 9.6 %copy-start.4 = (bf16[32,512]{1,0:T(8,128)(2,1)S(1)}, bf16[32,512]{1,0:T(8,128)(2,1)}, u32[]{:S(2)}) copy-start(bf16[32,512]{1,0:T(8,128)(2,1)} %param.20) | copy-start | bytes 98308
  23.7 4.1 %copy-start.11 = (f32[32]{0:T(128)S(1)}, f32[32]{0:T(128)}, u32[]{:S(2)}) copy-start(f32[32]{0:T(128)} %multiply_power_fusion) | copy-start | bytes 388
  29.3 5.4 %copy-start.1 = (bf16[32,576]{1,0:T(8,128)(2,1)}, bf16[32,576]{1,0:T(8,128)(2,1)S(1)}, u32[]{:S(2)}) copy-start(bf16[32,576]{1,0:T(8,128)(2,1)S(1)} %pad_maximum_fusion.3) | copy-start | bytes 110596
  33.1 18.2 %copy-start.7 = (s32[32,6]{0,1:T(8,128)S(1)}, s32[32,6]{0,1:T(8,128)}, u32[]{:S(2)}) copy-start(s32[32,6]{0,1:T(8,128)} %param.32) | copy-start | bytes 2308
  37.1 34.2 %all-to-all-start = ((bf16[64,6,576]{2,1,0:T(8,128)(2,1)}), bf16[64,6,576]{2,1,0:T(8,128)(2,1)}, u32[]{:S(2)}, u32[]{:S(2)}) async-start(bf16[64,6,576]{2,1,0:T(8,128)(2,1)} %pad_maximum_fusion), calls=%async_computation | async-start | bytes 1310720 | tf_op jit(solution)/shard_map/all_to_all | solution.py:165
  92.0 1.8 copy-start.12
  108.3 12.4 %all-to-all-start.1 = ((bf16[35,16,512]{2,0,1:T(8,128)(2,1)}), bf16[35,16,512]{2,0,1:T(8,128)(2,1)}, u32[]{:S(2)}, u32[]{:S(2)}) async-start(bf16[35,16,512]{2,0,1:T(8,128)(2,1)} %copy.314), calls=%async_computation.1 | async-start | bytes 1310720 | tf_op jit(solution)/shard_map/all_to_all | solution.py:186
  114.0 8.3 %copy-start.10 = (f32[32,1,4]{0,2,1:T(4,128)S(1)}, f32[32,1,4]{0,2,1:T(4,128)}, u32[]{:S(2)}) copy-start(f32[32,1,4]{0,2,1:T(4,128)} %copy.333) | copy-start | bytes 1540
  122.1 15.1 %copy-start.9 = (s32[384]{0:T(512)S(1)}, s32[384]{0:T(512)}, u32[]{:S(2)}) copy-start(s32[384]{0:T(512)} %get-tuple-element.30) | copy-start | bytes 4612
  127.8 19.1 %all-to-all-start.2 = ((bf16[64,2,256]{2,1,0:T(2,128)(2,1)}), bf16[64,2,256]{2,1,0:T(2,128)(2,1)S(1)}, u32[]{:S(2)}, u32[]{:S(2)}) async-start(bf16[64,2,256]{2,1,0:T(2,128)(2,1)} %reshape.670), calls=%async_computation.2 | async-start | bytes 131072 | tf_op jit(solution)/shard_map/all_to_all | solution.py:215
  147.6 11.1 %copy-start.5 = (bf16[512,64]{0,1:T(8,128)(2,1)S(1)}, bf16[512,64]{0,1:T(8,128)(2,1)}, u32[]{:S(2)}) copy-start(bf16[512,64]{0,1:T(8,128)(2,1)} %param.31) | copy-start | bytes 196612
  147.6 11.0 %copy-start.8 = (f32[512]{0:T(512)S(1)}, f32[512]{0:T(512)}, u32[]{:S(2)}) copy-start(f32[512]{0:T(512)} %param.30) | copy-start | bytes 6148
  150.4 8.1 %all-to-all-start.3 = ((bf16[32,4,512]{2,0,1:T(8,128)(2,1)}), bf16[32,4,512]{2,0,1:T(8,128)(2,1)S(1)}, u32[]{:S(2)}, u32[]{:S(2)}) async-start(bf16[32,4,512]{2,0,1:T(8,128)(2,1)} %bitcast.127), calls=%async_computation.3 | async-start | bytes 262144 | tf_op jit(solution)/shard_map/all_to_all | solution.py:54
  158.7 12.7 %copy-start.3 = (bf16[32,512]{1,0:T(8,128)(2,1)}, bf16[32,512]{1,0:T(8,128)(2,1)S(1)}, u32[]{:S(2)}) copy-start(bf16[32,512]{1,0:T(8,128)(2,1)S(1)} %get-tuple-element.38) | copy-start | bytes 98308
  206.5 24.2 %copy-start.13 = (bf16[1,2048,352]{1,2,0:T(8,128)(2,1)S(1)}, bf16[1,2048,352]{1,2,0:T(8,128)(2,1)}, u32[]{:S(2)}) copy-start(bf16[1,2048,352]{1,2,0:T(8,128)(2,1)} %param.33) | copy-start | bytes 4325380
  229.6 1.1 copy-start.2
  240.6 4.5 %copy-start.6 = (s32[32,6]{1,0:T(8,128)S(1)}, s32[32,6]{1,0:T(8,128)}, u32[]{:S(2)}) copy-start(s32[32,6]{1,0:T(8,128)} %get-tuple-element.35) | copy-start | bytes 2308
  240.6 24.1 %all-to-all-start.6 = ((bf16[384,4,512]{2,0,1:T(8,128)(2,1)}), bf16[384,4,512]{2,0,1:T(8,128)(2,1)}, u32[]{:S(2)}, u32[]{:S(2)}) async-start(bf16[384,4,512]{2,0,1:T(8,128)(2,1)} %bitcast.131), calls=%async_computation.6 | async-start | bytes 3145728 | tf_op jit(solution)/shard_map/all_to_all | solution.py:54
  267.4 25.3 %all-to-all-start.7 = ((bf16[64,6,512]{2,1,0:T(8,128)(2,1)}), bf16[64,6,512]{2,1,0:T(8,128)(2,1)}, u32[]{:S(2)}, u32[]{:S(2)}) async-start(bf16[64,6,512]{2,1,0:T(8,128)(2,1)} %reshape.557), calls=%async_computation.7 | async-start | bytes 1048576 | tf_op jit(solution)/shard_map/all_to_all | solution.py:277
where the time goes:
time: 301 us; the launch traced here: 299 us
  blocking collectives  87.5 us (29%)
  waiting for transfers between devices  72 us (24%)
  local copies, waits for them, and re-layouts  49.7 us (17%)
  starting transfers between devices  43.5 us (14%)
  matrix products  22.8 us (8%)
  other arithmetic  22.5 us (7%)
    all_to_all x1, blocking collectives, body(): lax.all_to_all(padded_rows[source_token].reshape(expert_count, capacity,...  27.4 us
    all_to_all x2, waiting for transfers between devices, head_sum_scatter(): lax.all_to_all(values, 'head', split_axis=axis, concat_axis=0, tiled=True)  24.3 us
    all_to_all x1, blocking collectives, body(): lax.all_to_all(jnp.broadcast_to(arrived.reshape(1, peer_count * capacity,...  23 us
    all_to_all x1, waiting for transfers between devices, body(): got_packed = lax.all_to_all(packed, 'tok', 0, 0, tiled=True)  16.5 us
    all_to_all x1, waiting for transfers between devices, body(): lax.all_to_all(expert_share.reshape(peer_count, capacity, quarter_width),...  15.5 us
    all_to_all x1, starting transfers between devices, body(): got_packed = lax.all_to_all(packed, 'tok', 0, 0, tiled=True)  14.2 us
    psum x1, blocking collectives, body(): lax.psum((jnp.sum(attended_wide * attended_wide, axis=1), jnp.dot(gained,...  12.5 us
    all_gather x1, blocking collectives, body(): got_rows = lax.all_gather(send_rows, 'head', axis=0, tiled=False)  12.5 us
  transfers between devices with their start and end apart: 6, of which 6 were waited for; matrix products, arithmetic and copies ran while one was open for 3% of the time, Pallas kernels for 0%

commit v1 on v0

--- a/solution.py
+++ b/solution.py
@@ -172,7 +172,12 @@
     owner_probes = got_packed[src_of_slot, :local_heads]
     owner_lengths = got_len[src_of_slot]
     owner_new = got_packed[src_of_slot, local_heads]
-    all_heads = lax.all_gather(owner_probes, "head", axis=1, tiled=True)
+    all_heads = jnp.concatenate(
+        lax.all_to_all(
+            jnp.stack([owner_probes for _ in range(lax.axis_size("head"))], axis=0), "head", 0, 0
+        ),
+        1,
+    )
     numerator, denominator = owner_attend(
         all_heads, owner_lengths, latent_cache, head_index, factor
     )

time: 301 us -> 311 us (1.033)
  blocking collectives: 87.5 us -> 75.2 us
  waiting for transfers between devices: 72 us -> 80.5 us
  local copies, waits for them, and re-layouts: 49.7 us -> 56 us
    all_gather x1 -> x0, blocking collectives: 12.1 us -> none  [body(): all_heads = lax.all_gather(owner_probes, 'head', axis=1, tiled=True)]
    all_to_all x0 -> x1, waiting for transfers between devices: none -> 7.48 us  [body(): lax.all_to_all(jnp.stack([owner_probes for _ in range(lax.axis_size('head...]
    all_to_all x0 -> x1, starting transfers between devices: none -> 4.34 us  [body(): lax.all_to_all(jnp.stack([owner_probes for _ in range(lax.axis_size('head...]
    another operation x1 -> x3, local copies, waits for them, and re-layouts: 0.09 us -> 3.34 us  [the longest x1 2.24 us: owner_attend(): all_heads.reshape(slot_rows * total_heads, probe_width)]
  transfers between devices with their start and end apart: 6 -> 7, of which waited for: 6 -> 7; matrix products, arithmetic and copies ran while one was open for 3% -> 4% of each run, Pallas kernels for 0% -> 0%
where the time goes in v1:
time: 311 us; the launch traced here: 309 us
  waiting for transfers between devices  80.5 us (26%)
  blocking collectives  75.2 us (24%)
  local copies, waits for them, and re-layouts  56 us (18%)
  starting transfers between devices  46.4 us (15%)
  matrix products  25.1 us (8%)
  other arithmetic  24.2 us (8%)
    all_to_all x1, blocking collectives, body(): lax.all_to_all(padded_rows[source_token].reshape(expert_count, capacity,...  27.4 us
    all_to_all x2, waiting for transfers between devices, head_sum_scatter(): lax.all_to_all(values, 'head', split_axis=axis, concat_axis=0, tiled=True)  24.3 us
    all_to_all x1, blocking collectives, body(): lax.all_to_all(jnp.broadcast_to(arrived.reshape(1, peer_count * capacity,...  23 us
    all_to_all x1, waiting for transfers between devices, body(): got_packed = lax.all_to_all(packed, 'tok', 0, 0, tiled=True)  15.9 us
    all_to_all x1, waiting for transfers between devices, body(): lax.all_to_all(expert_share.reshape(peer_count, capacity, quarter_width),...  15.5 us
    all_to_all x1, starting transfers between devices, body(): got_packed = lax.all_to_all(packed, 'tok', 0, 0, tiled=True)  14.2 us
    all_gather x1, blocking collectives, body(): got_rows = lax.all_gather(send_rows, 'head', axis=0, tiled=False)  12.5 us
    psum x1, blocking collectives, body(): lax.psum((jnp.sum(attended_wide * attended_wide, axis=1), jnp.dot(gained,...  12.3 us
  transfers between devices with their start and end apart: 7, of which 7 were waited for; matrix products, arithmetic and copies ran while one was open for 4% of the time, Pallas kernels for 0%

profile of v1, /device:TPU:1, one launch (start us, length us, event | category | flops | bytes accessed | tf_op | source)
XLA Modules:
  0.0 308.6 jit_solution(17066194232825080103)
XLA Ops:
  10.4 12.5 %all-gather = bf16[128,2432]{1,0:T(8,128)(2,1)S(1)} all-gather(bf16[32,2432]{1,0:T(8,128)(2,1)S(1)} %concatenate.36), channel_id=2, replica_groups=mesh['tok'=64,'head'=4] {'head'}, dimensions={0}, use_global_device_ids=true | all-gather | bytes 778240 | tf_op jit(solution)/shard_map/all_gather | solution.py:110
  34.7 2.5 pad_maximum_fusion
  37.1 14.2 %all-to-all-start = ((bf16[64,6,576]{2,1,0:T(8,128)(2,1)}), bf16[64,6,576]{2,1,0:T(8,128)(2,1)}, u32[]{:S(2)}, u32[]{:S(2)}) async-start(bf16[64,6,576]{2,1,0:T(8,128)(2,1)} %pad_maximum_fusion), calls=%async_computation | async-start | bytes 1310720 | tf_op jit(solution)/shard_map/all_to_all | solution.py:165
  55.4 15.9 %all-to-all-done = bf16[64,6,576]{2,1,0:T(8,128)(2,1)} async-done(((bf16[64,6,576]{2,1,0:T(8,128)(2,1)}), bf16[64,6,576]{2,1,0:T(8,128)(2,1)}, u32[]{:S(2)}, u32[]{:S(2)}) %all-to-all-start) | async-done | bytes 442400 | tf_op jit(solution)/shard_map/all_to_all | solution.py:165
  74.8 1.9 copy.313
  78.5 2.1 gather_fusion.5
  81.8 4.3 %all-to-all-start.1 = ((bf16[4,32,4,576]{3,2,1,0:T(4,128)(2,1)}), bf16[4,32,4,576]{3,2,1,0:T(4,128)(2,1)}, u32[]{:S(2)}, u32[]{:S(2)}) async-start(bf16[4,32,4,576]{3,2,1,0:T(4,128)(2,1)} %stack.35), calls=%async_computation.1 | async-start | bytes 1310720 | tf_op jit(solution)/shard_map/all_to_all | solution.py:176
  86.7 2.5 copy.318
  89.1 7.5 %all-to-all-done.1 = bf16[4,32,4,576]{3,2,1,0:T(4,128)(2,1)} async-done(((bf16[4,32,4,576]{3,2,1,0:T(4,128)(2,1)}), bf16[4,32,4,576]{3,2,1,0:T(4,128)(2,1)}, u32[]{:S(2)}, u32[]{:S(2)}) %all-to-all-start.1) | async-done | bytes 589856 | tf_op jit(solution)/shard_map/all_to_all | solution.py:176
  96.6 2.1 copy.315
  98.8 2.2 reshape_reshape.3
  101.0 6.8 %convert_reduce_fusion = (f32[512]{0:T(512)S(1)}, bf16[512,2496]{0,1:T(8,128)(2,1)}) fusion(pred[512,2496]{0,1:T(32,128)(4,1)} %copy.318, bf16[512,576]{1,0:T(8,128)(2,1)} %reshape_reshape.3, bf16[2496,576]{0,1:T(8,128)(2,1)} %param.27), kind=kOutput, calls=%fused_computation.13 | convolution fusion | flops 1478589952 | bytes 7301120 | tf_op jit(solution)/shard_map/qc,pc->qp/dot_general | solution.py:37
  108.0 4.4 %copy.316 = bf16[512,2496]{1,0:T(8,128)(2,1)} copy(bf16[512,2496]{0,1:T(8,128)(2,1)} %get-tuple-element.67) | data formatting | bytes 5111808 | tf_op jit(solution)/shard_map/exp | solution.py:44
  112.4 4.1 %fusion.10 = bf16[32,16,512]{2,1,0:T(8,128)(2,1)S(1)} fusion(bf16[2496,576]{0,1:T(8,128)(2,1)} %param.27, bf16[32,16,2496]{2,1,0:T(8,128)(2,1)} %bitcast.139, pred[32,2496]{1,0:T(8,128)(4,1)S(1)} %compare_and_fusion), kind=kOutput, calls=%fused_computation.29 | convolution fusion | flops 1310162944 | bytes 5847040 | tf_op jit(solution)/shard_map/khp,pl->khl/dot_general | solution.py:45
  117.8 4.2 %all-to-all-start.2 = ((bf16[35,16,512]{2,0,1:T(8,128)(2,1)}), bf16[35,16,512]{2,0,1:T(8,128)(2,1)}, u32[]{:S(2)}, u32[]{:S(2)}) async-start(bf16[35,16,512]{2,0,1:T(8,128)(2,1)} %copy.320), calls=%async_computation.2 | async-start | bytes 1310720 | tf_op jit(solution)/shard_map/all_to_all | solution.py:191
  123.5 8.2 %all-to-all-done.2 = bf16[35,16,512]{2,0,1:T(8,128)(2,1)} async-done(((bf16[35,16,512]{2,0,1:T(8,128)(2,1)}), bf16[35,16,512]{2,0,1:T(8,128)(2,1)}, u32[]{:S(2)}, u32[]{:S(2)}) %all-to-all-start.2) | async-done | bytes 573472 | tf_op jit(solution)/shard_map/all_to_all | solution.py:191
  138.9 7.8 %all-to-all-start.3 = ((bf16[64,2,256]{2,1,0:T(2,128)(2,1)}), bf16[64,2,256]{2,1,0:T(2,128)(2,1)S(1)}, u32[]{:S(2)}, u32[]{:S(2)}) async-start(bf16[64,2,256]{2,1,0:T(2,128)(2,1)} %reshape.672), calls=%async_computation.3 | async-start | bytes 131072 | tf_op jit(solution)/shard_map/all_to_all | solution.py:220
  147.4 9.1 %all-to-all-done.3 = bf16[64,2,256]{2,1,0:T(2,128)(2,1)S(1)} async-done(((bf16[64,2,256]{2,1,0:T(2,128)(2,1)}), bf16[64,2,256]{2,1,0:T(2,128)(2,1)S(1)}, u32[]{:S(2)}, u32[]{:S(2)}) %all-to-all-start.3) | async-done | bytes 65568 | tf_op jit(solution)/shard_map/all_to_all | solution.py:220
  157.2 2.1 convolution_convert_fusion.1
  160.0 3.3 %all-to-all-start.4 = ((bf16[32,4,512]{2,0,1:T(8,128)(2,1)}), bf16[32,4,512]{2,0,1:T(8,128)(2,1)S(1)}, u32[]{:S(2)}, u32[]{:S(2)}) async-start(bf16[32,4,512]{2,0,1:T(8,128)(2,1)} %bitcast.128), calls=%async_computation.4 | async-start | bytes 262144 | tf_op jit(solution)/shard_map/all_to_all | solution.py:54
  163.3 4.8 %all-to-all-done.4 = bf16[32,4,512]{2,0,1:T(8,128)(2,1)S(1)} async-done(((bf16[32,4,512]{2,0,1:T(8,128)(2,1)}), bf16[32,4,512]{2,0,1:T(8,128)(2,1)S(1)}, u32[]{:S(2)}, u32[]{:S(2)}) %all-to-all-start.4) | async-done | bytes 131104 | tf_op jit(solution)/shard_map/all_to_all | solution.py:54
  168.4 12.3 %all-reduce.6 = (f32[32]{0:T(128)S(1)}, f32[32,64]{1,0:T(8,128)}) all-reduce(f32[32]{0:T(128)S(1)} %get-tuple-element.37, f32[32,64]{1,0:T(8,128)S(1)} %fusion.55), channel_id=1, replica_groups=mesh['tok'=64,'head'=4] {'head'}, use_global_device_ids=true, to_apply=%region_14.15 | all-reduce | flops 2080 | bytes 16640 | tf_op jit(solution)/shard_map/psum | solution.py:228
  180.8 2.6 gather_fusion.9
  183.3 1.9 reshape.557
  185.3 27.4 %all_to_all.82 = bf16[64,6,512]{2,1,0:T(8,128)(2,1)} all-to-all(bf16[64,6,512]{2,1,0:T(8,128)(2,1)} %reshape.557), channel_id=1, replica_groups=mesh['tok'=64,'head'=4] {'tok'}, dimensions={0} | all-to-all | bytes 786432 | tf_op jit(solution)/shard_map/all_to_all | solution.py:258
  215.9 23.0 %all_to_all.83 = bf16[4,384,512]{1,2,0:T(8,128)(2,1)S(1)} all-to-all(bf16[4,384,512]{1,2,0:T(8,128)(2,1)S(1)} %broadcast_in_dim.157), channel_id=1, replica_groups=mesh['tok'=64,'head'=4] {'head'}, dimensions={0} | all-to-all | bytes 3145728 | tf_op jit(solution)/shard_map/all_to_all | solution.py:265
  241.8 5.5 %convolution_convert_fusion = bf16[384,2048]{1,0:T(8,128)(2,1)} fusion(bf16[1,352,2048]{2,1,0:T(8,128)(2,1)} %param.35, bf16[384,2048]{0,1:T(8,128)(2,1)} %bitcast.142, bf16[1,2048,352]{1,2,0:T(8,128)(2,1)} %param.34, f32[384,352]{0,1:T(8,128)} %fusion.8), kind=kOutput, calls=%fused_computation.16 | convolution fusion | flops 1108893696 | bytes 6569984 | tf_op jit(solution)/shard_map/dot_general | solution.py:279
  247.3 2.7 copy.360
  250.0 4.5 %all-to-all-start.7 = ((bf16[384,4,512]{2,0,1:T(8,128)(2,1)}), bf16[384,4,512]{2,0,1:T(8,128)(2,1)}, u32[]{:S(2)}, u32[]{:S(2)}) async-start(bf16[384,4,512]{2,0,1:T(8,128)(2,1)} %bitcast.132), calls=%async_computation.7 | async-start | bytes 3145728 | tf_op jit(solution)/shard_map/all_to_all | solution.py:54
  254.6 19.5 %all-to-all-done.7 = bf16[384,4,512]{2,0,1:T(8,128)(2,1)} async-done(((bf16[384,4,512]{2,0,1:T(8,128)(2,1)}), bf16[384,4,512]{2,0,1:T(8,128)(2,1)}, u32[]{:S(2)}, u32[]{:S(2)}) %all-to-all-start.7) | async-done | bytes 1572896 | tf_op jit(solution)/shard_map/all_to_all | solution.py:54
  276.8 8.1 %all-to-all-start.8 = ((bf16[64,6,512]{2,1,0:T(8,128)(2,1)}), bf16[64,6,512]{2,1,0:T(8,128)(2,1)}, u32[]{:S(2)}, u32[]{:S(2)}) async-start(bf16[64,6,512]{2,1,0:T(8,128)(2,1)} %reshape.559), calls=%async_computation.8 | async-start | bytes 1048576 | tf_op jit(solution)/shard_map/all_to_all | solution.py:282
  286.6 15.5 %all-to-all-done.8 = bf16[64,6,512]{2,1,0:T(8,128)(2,1)} async-done(((bf16[64,6,512]{2,1,0:T(8,128)(2,1)}), bf16[64,6,512]{2,1,0:T(8,128)(2,1)}, u32[]{:S(2)}, u32[]{:S(2)}) %all-to-all-start.8) | async-done | bytes 393248 | tf_op jit(solution)/shard_map/all_to_all | solution.py:282
  (167 shorter events, 61.9 us)
Async XLA Ops:
  0.6 23.1 %copy-start = (bf16[2048,768]{1,0:T(8,128)(2,1)S(1)}, bf16[2048,768]{1,0:T(8,128)(2,1)}, u32[]{:S(2)}) copy-start(bf16[2048,768]{1,0:T(8,128)(2,1)} %param.22) | copy-start | bytes 9437188
  0.6 9.6 %copy-start.4 = (bf16[32,512]{1,0:T(8,128)(2,1)S(1)}, bf16[32,512]{1,0:T(8,128)(2,1)}, u32[]{:S(2)}) copy-start(bf16[32,512]{1,0:T(8,128)(2,1)} %param.20) | copy-start | bytes 98308
  23.7 4.1 %copy-start.16 = (f32[32]{0:T(128)S(1)}, f32[32]{0:T(128)}, u32[]{:S(2)}) copy-start(f32[32]{0:T(128)} %multiply_power_fusion) | copy-start | bytes 388
  29.3 5.3 %copy-start.1 = (bf16[32,576]{1,0:T(8,128)(2,1)}, bf16[32,576]{1,0:T(8,128)(2,1)S(1)}, u32[]{:S(2)}) copy-start(bf16[32,576]{1,0:T(8,128)(2,1)S(1)} %pad_maximum_fusion.3) | copy-start | bytes 110596
  33.1 18.2 %copy-start.8 = (s32[32,6]{0,1:T(8,128)S(1)}, s32[32,6]{0,1:T(8,128)}, u32[]{:S(2)}) copy-start(s32[32,6]{0,1:T(8,128)} %param.32) | copy-start | bytes 2308
  37.1 34.2 %all-to-all-start = ((bf16[64,6,576]{2,1,0:T(8,128)(2,1)}), bf16[64,6,576]{2,1,0:T(8,128)(2,1)}, u32[]{:S(2)}, u32[]{:S(2)}) async-start(bf16[64,6,576]{2,1,0:T(8,128)(2,1)} %pad_maximum_fusion), calls=%async_computation | async-start | bytes 1310720 | tf_op jit(solution)/shard_map/all_to_all | solution.py:165
  74.2 4.3 %copy-start.13 = (s32[32]{0:T(128)}, s32[32]{0:T(128)S(1)}, u32[]{:S(2)}) copy-start(s32[32]{0:T(128)S(1)} %reduce.18) | copy-start | bytes 388
  80.8 5.4 %copy-start.7 = (s32[2496]{0:T(1024)S(1)}, s32[2496]{0:T(1024)}, u32[]{:S(2)}) copy-start(s32[2496]{0:T(1024)} %iota_add_fusion) | copy-start | bytes 29956
  80.8 5.4 %copy-start.14 = (s32[32]{0:T(128)S(1)}, s32[32]{0:T(128)}, u32[]{:S(2)}) copy-start(s32[32]{0:T(128)} %copy-done.13) | copy-start | bytes 388
  80.8 5.4 %copy-start.15 = (s32[32]{0:T(128)S(1)}, s32[32]{0:T(128)}, u32[]{:S(2)}) copy-start(s32[32]{0:T(128)} %sub.82) | copy-start | bytes 388
  81.8 14.8 %all-to-all-start.1 = ((bf16[4,32,4,576]{3,2,1,0:T(4,128)(2,1)}), bf16[4,32,4,576]{3,2,1,0:T(4,128)(2,1)}, u32[]{:S(2)}, u32[]{:S(2)}) async-start(bf16[4,32,4,576]{3,2,1,0:T(4,128)(2,1)} %stack.35), calls=%async_computation.1 | async-start | bytes 1310720 | tf_op jit(solution)/shard_map/all_to_all | solution.py:176
  116.6 6.3 %copy-start.12 = (s32[64]{0:T(128)S(1)}, s32[64]{0:T(128)}, u32[]{:S(2)}) copy-start(s32[64]{0:T(128)} %get-tuple-element.27) | copy-start | bytes 772
  117.8 13.9 %all-to-all-start.2 = ((bf16[35,16,512]{2,0,1:T(8,128)(2,1)}), bf16[35,16,512]{2,0,1:T(8,128)(2,1)}, u32[]{:S(2)}, u32[]{:S(2)}) async-start(bf16[35,16,512]{2,0,1:T(8,128)(2,1)} %copy.320), calls=%async_computation.2 | async-start | bytes 1310720 | tf_op jit(solution)/shard_map/all_to_all | solution.py:191
  123.5 9.9 %copy-start.11 = (f32[32,1,4]{0,2,1:T(4,128)S(1)}, f32[32,1,4]{0,2,1:T(4,128)}, u32[]{:S(2)}) copy-start(f32[32,1,4]{0,2,1:T(4,128)} %copy.338) | copy-start | bytes 1540
  133.1 13.6 %copy-start.10 = (s32[384]{0:T(512)S(1)}, s32[384]{0:T(512)}, u32[]{:S(2)}) copy-start(s32[384]{0:T(512)} %get-tuple-element.30) | copy-start | bytes 4612
  138.9 17.6 %all-to-all-start.3 = ((bf16[64,2,256]{2,1,0:T(2,128)(2,1)}), bf16[64,2,256]{2,1,0:T(2,128)(2,1)S(1)}, u32[]{:S(2)}, u32[]{:S(2)}) async-start(bf16[64,2,256]{2,1,0:T(2,128)(2,1)} %reshape.672), calls=%async_computation.3 | async-start | bytes 131072 | tf_op jit(solution)/shard_map/all_to_all | solution.py:220
  157.2 11.1 %copy-start.5 = (bf16[512,64]{0,1:T(8,128)(2,1)S(1)}, bf16[512,64]{0,1:T(8,128)(2,1)}, u32[]{:S(2)}) copy-start(bf16[512,64]{0,1:T(8,128)(2,1)} %param.31) | copy-start | bytes 196612
  157.2 11.0 %copy-start.9 = (f32[512]{0:T(512)S(1)}, f32[512]{0:T(512)}, u32[]{:S(2)}) copy-start(f32[512]{0:T(512)} %param.30) | copy-start | bytes 6148
  160.0 8.1 %all-to-all-start.4 = ((bf16[32,4,512]{2,0,1:T(8,128)(2,1)}), bf16[32,4,512]{2,0,1:T(8,128)(2,1)S(1)}, u32[]{:S(2)}, u32[]{:S(2)}) async-start(bf16[32,4,512]{2,0,1:T(8,128)(2,1)} %bitcast.128), calls=%async_computation.4 | async-start | bytes 262144 | tf_op jit(solution)/shard_map/all_to_all | solution.py:54
  168.3 12.4 %copy-start.3 = (bf16[32,512]{1,0:T(8,128)(2,1)}, bf16[32,512]{1,0:T(8,128)(2,1)S(1)}, u32[]{:S(2)}) copy-start(bf16[32,512]{1,0:T(8,128)(2,1)S(1)} %get-tuple-element.38) | copy-start | bytes 98308
  215.9 24.2 %copy-start.17 = (bf16[1,2048,352]{1,2,0:T(8,128)(2,1)S(1)}, bf16[1,2048,352]{1,2,0:T(8,128)(2,1)}, u32[]{:S(2)}) copy-start(bf16[1,2048,352]{1,2,0:T(8,128)(2,1)} %param.33) | copy-start | bytes 4325380
  239.0 1.1 copy-start.2
  250.0 4.5 %copy-start.6 = (s32[32,6]{1,0:T(8,128)S(1)}, s32[32,6]{1,0:T(8,128)}, u32[]{:S(2)}) copy-start(s32[32,6]{1,0:T(8,128)} %get-tuple-element.35) | copy-start | bytes 2308
  250.0 24.1 %all-to-all-start.7 = ((bf16[384,4,512]{2,0,1:T(8,128)(2,1)}), bf16[384,4,512]{2,0,1:T(8,128)(2,1)}, u32[]{:S(2)}, u32[]{:S(2)}) async-start(bf16[384,4,512]{2,0,1:T(8,128)(2,1)} %bitcast.132), calls=%async_computation.7 | async-start | bytes 3145728 | tf_op jit(solution)/shard_map/all_to_all | solution.py:54
  276.8 25.3 %all-to-all-start.8 = ((bf16[64,6,512]{2,1,0:T(8,128)(2,1)}), bf16[64,6,512]{2,1,0:T(8,128)(2,1)}, u32[]{:S(2)}, u32[]{:S(2)}) async-start(bf16[64,6,512]{2,1,0:T(8,128)(2,1)} %reshape.559), calls=%async_computation.8 | async-start | bytes 1048576 | tf_op jit(solution)/shard_map/all_to_all | solution.py:282
